TPU v7x, 256 devices: a whole 4x4x8 slice. The times are simulated.
256 devices in a mesh: row: 16 (over x_hi, z), col: 16 (over x_lo, y, core).
Axes of the slice: x: 4 (x_hi: 2, x_lo: 2; x = x_hi * 2 + x_lo), y: 4, z: 8, core: 2. Of those that a mesh axis runs over, the one named last changes fastest.
Arguments:
- features: bfloat16 [3, 256, 256, 1024], P(None, 'row', 'col'), may hold values from -6 to 6
- dw_kernel: bfloat16 [7, 7, 1024], replicated, may hold values from -0.875 to 0.875
- ln_gain: float32 [1024], replicated, may hold values from 0.1 to 1.9
- w_in: bfloat16 [1024, 4096], P(None, 'col'), may hold values from -0.1875 to 0.1875
- w_down: bfloat16 [1024, 4096], P(None, 'col'), may hold values from -0.09375 to 0.09375
- gamma: float32 [1024], replicated, may hold values from 0.3 to 1.5
- labels: int32 [3, 256, 256], P(None, 'row', 'col'), may hold values from 0 to 15
- valid: int32 [3, 256, 256], P(None, 'row', 'col'), may hold values 0 or 1
Outputs:
- gram: float32 [1024, 1024], P(('row', 'col'))
- cross: float32 [1024, 16], P(('row', 'col'))
All inputs are finite; a program needn't handle non-finite values. No bound on the sum of `valid` on one device may be relied on, other than what follows from the above.
Results may differ from a plain program's by a relative error of at most 0.0037.
Values may be sent and summed in bfloat16 or wider, within the bound.
No kernel may reach another device: no remote copies, remote signals or barrier semaphores. Data moves between devices by JAX's collectives and lax.ppermute only.
A program may use at most 128 MiB of HBM per device.

v0:
```python
import jax
import jax.numpy as jnp
from jax import lax
from jax.sharding import PartitionSpec as P

NCLS = 16
KSIZE = 7


def with_halo(shard, sides, width):
    for axis, dim in sides:
        size, length = (lax.axis_size(axis), shard.shape[dim])
        up = [(i, (i + 1) % size) for i in range(size - 1)]
        down = [(j, i) for i, j in up]
        last = lax.slice_in_dim(shard, length - width, length, axis=dim)
        leading = lax.slice_in_dim(shard, 0, width, axis=dim)
        before = lax.ppermute(last, axis, up)
        after = lax.ppermute(leading, axis, down)
        shard = jnp.concatenate([before, shard, after], axis=dim)
    return shard


def apply_norm(rows, ln_gain):
    mean = jnp.mean(rows, axis=-1, keepdims=True)
    centered = rows - mean
    var = jnp.mean(centered * centered, axis=-1, keepdims=True)
    return (centered * lax.rsqrt(var + 1e-06) * ln_gain).astype(jnp.bfloat16)


def expand(normed, piece):
    return jax.nn.gelu(
        jnp.dot(normed, piece, preferred_element_type=jnp.float32), approximate=False
    ).astype(jnp.bfloat16)


def contract(hidden, piece):
    return lax.dot_general(
        hidden, piece, (((1,), (1,)), ((), ())), preferred_element_type=jnp.float32
    )


def on_device(features, dw_kernel, ln_gain, w_in, w_down, gamma, labels, valid):
    tiles, high, wide, width = features.shape
    padded = with_halo(features, (("row", 1), ("col", 2)), 3).astype(jnp.float32)
    kernel = dw_kernel.astype(jnp.float32)
    conv = jnp.zeros((tiles, high, wide, width), jnp.float32)
    for i in range(KSIZE):
        for j in range(KSIZE):
            conv = conv + padded[:, i : i + high, j : j + wide, :] * kernel[i, j]
    count = tiles * high * wide
    normed = apply_norm(conv.reshape(count, width), ln_gain)
    hidden = expand(normed, lax.all_gather(w_in, "col", axis=1, tiled=True))
    branch = contract(hidden, lax.all_gather(w_down, "col", axis=1, tiled=True))
    out = (features.reshape(count, width).astype(jnp.float32) + gamma * branch).astype(jnp.bfloat16)
    keep = valid.reshape(count, 1)
    masked = out * keep.astype(jnp.bfloat16)
    classes = jnp.arange(NCLS, dtype=jnp.int32)
    onehot = (labels.reshape(count, 1) == classes[None, :]).astype(jnp.float32)
    targets = ((onehot - 1.0 / NCLS) * keep.astype(jnp.float32)).astype(jnp.bfloat16)
    gram_part = lax.dot_general(
        masked, out, (((0,), (0,)), ((), ())), preferred_element_type=jnp.float32
    )
    cross_part = lax.dot_general(
        out, targets, (((0,), (0,)), ((), ())), preferred_element_type=jnp.float32
    )
    gram_sum, cross_sum = (
        lax.psum_scatter(gram_part, ("row", "col"), scatter_dimension=0, tiled=True),
        lax.psum_scatter(cross_part, ("row", "col"), scatter_dimension=0, tiled=True),
    )
    total = float(tiles * high * lax.axis_size("row") * wide * lax.axis_size("col"))
    return (gram_sum / total, cross_sum / jnp.sqrt(jnp.float32(total)))


def solution(mesh):
    return jax.shard_map(
        on_device,
        mesh=mesh,
        in_specs=(
            P(None, "row", "col", None),
            P(),
            P(),
            P(None, "col"),
            P(None, "col"),
            P(),
            P(None, "row", "col"),
            P(None, "row", "col"),
        ),
        out_specs=(P(("row", "col"), None), P(("row", "col"), None)),
        check_vma=False,
    )
```

profile of v0, /device:TPU:120, one launch (start us, length us, event | category | flops | bytes accessed | tf_op | source)
XLA Modules:
  0.0 479.2 jit_solution(6179449050125155044)
XLA Ops:
  7.2 0.7 all-gather.3.cloned.1.call-update
  8.0 1.1 fusion.107
  9.1 5.0 %collective-permute-start = (bf16[3,3,16,1024]{3,2,1,0:T(8,128)(2,1)S(1)}, bf16[3,3,16,1024]{3,2,1,0:T(8,128)(2,1)S(1)}, u32[]{:S(2)}, u32[]{:S(2)}) collective-permute-start(bf16[3,3,16,1024]{3,2,1,0:T(8,128)(2,1)S(1)} %get-tuple-element.9), channel_id=1, source_target_pairs={{0,16},{16,32},{32,48},{48,64},{64,80},{80,96},{96,112},{112,128},... | collective-permute-start | bytes 884744 | tf_op jit(solution)/shard_map/ppermute | solution.py:17
  14.1 1.9 collective-permute-start.1
  16.1 1.2 fusion.108
  17.3 0.8 fusion.111
  18.1 0.7 convert_element_type.57
  18.8 0.7 convert_element_type.60
  19.4 1.4 eq.15
  21.1 4.6 collective-permute-done.1
  26.4 1.9 collective-permute-start.2
  28.5 3.6 collective-permute-start.3
  32.2 9.4 %collective-permute-done.2 = bf16[3,22,3,1024]{3,1,2,0:T(8,128)(2,1)S(1)} collective-permute-done((bf16[3,22,3,1024]{3,1,2,0:T(8,128)(2,1)S(1)}, bf16[3,22,3,1024]{3,1,2,0:T(8,128)(2,1)S(1)}, u32[]{:S(2)}, u32[]{:S(2)}) %collective-permute-start.2) | collective-permute-done | bytes 405536 | tf_op jit(solution)/shard_map/ppermute | solution.py:17
  41.9 4.8 %collective-permute-done.3 = bf16[3,22,3,1024]{3,1,2,0:T(8,128)(2,1)S(1)} collective-permute-done((bf16[3,22,3,1024]{3,1,2,0:T(8,128)(2,1)S(1)}, bf16[3,22,3,1024]{3,1,2,0:T(8,128)(2,1)S(1)}, u32[]{:S(2)}, u32[]{:S(2)}) %collective-permute-start.3) | collective-permute-done | bytes 405536 | tf_op jit(solution)/shard_map/ppermute | solution.py:18
  47.1 4.3 maximum_convert_fusion
  51.4 92.9 %fusion.104 = (f32[3,16,16]{2,1,0:T(8,128)S(1)}, f32[3,16,16,1024]{3,2,1,0:T(8,128)S(1)}) fusion(f32[1024]{0:T(1024)S(1)} %bitcast.102, f32[3,22,22,1024]{3,2,1,0:T(8,128)} %maximum_convert_fusion, f32[1024]{0:T(1024)S(1)} %bitcast.101, f32[1024]{0:T(1024)S(1)} %bitcast.100, f32[1024]{0:T(1024)S(1)} %bitcast.99, f32[1024]{0:T(1024)S(1)} %bitcast.98, ...), kind=kLoop, calls=%fused_computation.172 | loop fusion | flops 77069568 | bytes 157490176 | tf_op jit(solution)/shard_map/reduce_sum | solution.py:24
  145.0 1.6 fusion.63
  146.6 36.3 %fusion.128 = bf16[768,4096]{1,0:T(8,128)(2,1)} fusion(bf16[768,1024]{1,0:T(8,128)(2,1)} %fusion.63, bf16[1024,4096]{1,0:T(8,128)(2,1)} %all-gather.3.cloned.1.call-done), kind=kOutput, calls=%fused_computation.3.clone.clone.clone.clone.1 | convolution fusion | flops 6646923264 | bytes 16252928 | tf_op jit(solution)/shard_map/dot_general | solution.py:32
  182.9 11.2 %fusion.60 = bf16[768,1024]{1,0:T(8,128)(2,1)S(1)} fusion(bf16[768,1024]{1,0:T(8,128)(2,1)S(1)} %bitcast.72, bf16[1024,4096]{1,0:T(8,128)(2,1)} %all-gather.5.cloned.1.call-done, f32[1024]{0:T(1024)S(1)} %copy-done.7, bf16[768,4096]{1,0:T(8,128)(2,1)} %fusion.128), kind=kOutput, calls=%fused_computation.119 | convolution fusion | flops 6445596672 | bytes 17829888 | tf_op jit(solution)/shard_map/dot_general | solution.py:37
  194.2 3.9 fusion.64
  198.1 1.4 fusion.69
  199.6 270.5 %all-reduce.5.cloned.1.call-done = (f32[1024,1024]{1,0:T(8,128)}, f32[1024,16]{1,0:T(8,128)}) async-done(((f32[1024,1024]{1,0:T(8,128)}, f32[1024,16]{1,0:T(8,128)}), (f32[1024,1024]{1,0:T(8,128)}, f32[1024,16]{1,0:T(8,128)})) %all-reduce.5.cloned.1.call-update) | async-done | bytes 4259856
  470.0 1.4 dynamic-slice_multiply_fusion
  471.4 1.3 dynamic-slice_multiply_fusion.1
  (39 shorter events, 2.7 us)
Async XLA Ops:
  7.2 13.7 %copy-start = (bf16[3,16,16,1024]{3,2,1,0:T(8,128)(2,1)S(1)}, bf16[3,16,16,1024]{3,2,1,0:T(8,128)(2,1)}, u32[]{:S(2)}) copy-start(bf16[3,16,16,1024]{3,2,1,0:T(8,128)(2,1)} %param.8) | copy-start | bytes 4718596
  7.2 139.4 %all-gather.3.cloned.1.call-start = ((), (), s32[]{:S(2)}) async-start(), calls=%async_computation | async-start | bytes 8912896 | tf_op jit(solution)/shard_map/all_gather | solution.py:52
  7.9 175.0 %all-gather.5.cloned.1.call-start = ((), (), s32[]{:S(2)}) async-start(), calls=%async_computation.1 | async-start | bytes 8912896 | tf_op jit(solution)/shard_map/all_gather | solution.py:53
  9.1 11.8 %collective-permute-start = (bf16[3,3,16,1024]{3,2,1,0:T(8,128)(2,1)S(1)}, bf16[3,3,16,1024]{3,2,1,0:T(8,128)(2,1)S(1)}, u32[]{:S(2)}, u32[]{:S(2)}) collective-permute-start(bf16[3,3,16,1024]{3,2,1,0:T(8,128)(2,1)S(1)} %get-tuple-element.9), channel_id=1, source_target_pairs={{0,16},{16,32},{32,48},{48,64},{64,80},{80,96},{96,112},{112,128},... | collective-permute-start | bytes 884744 | tf_op jit(solution)/shard_map/ppermute | solution.py:17
  14.1 11.6 %collective-permute-start.1 = (bf16[3,3,16,1024]{3,2,1,0:T(8,128)(2,1)S(1)}, bf16[3,3,16,1024]{3,2,1,0:T(8,128)(2,1)S(1)}, u32[]{:S(2)}, u32[]{:S(2)}) collective-permute-start(bf16[3,3,16,1024]{3,2,1,0:T(8,128)(2,1)S(1)} %get-tuple-element.8), channel_id=1, source_target_pairs={{16,0},{32,16},{48,32},{64,48},{80,64},{96,80},{112,96},{128,112},... | collective-permute-start | bytes 884744 | tf_op jit(solution)/shard_map/ppermute | solution.py:18
  16.1 454.0 %all-reduce.5.cloned.1.call-start = ((), (), s32[]{:S(2)}) async-start(), calls=%async_computation.2 | async-start | bytes 9437184
  21.1 11.0 %copy-start.2 = (bf16[7,7,1024]{2,1,0:T(8,128)(2,1)S(1)}, bf16[7,7,1024]{2,1,0:T(8,128)(2,1)}, u32[]{:S(2)}) copy-start(bf16[7,7,1024]{2,1,0:T(8,128)(2,1)} %param.9) | copy-start | bytes 301060
  26.4 15.2 %collective-permute-start.2 = (bf16[3,22,3,1024]{3,1,2,0:T(8,128)(2,1)S(1)}, bf16[3,22,3,1024]{3,1,2,0:T(8,128)(2,1)S(1)}, u32[]{:S(2)}, u32[]{:S(2)}) collective-permute-start(bf16[3,22,3,1024]{3,1,2,0:T(8,128)(2,1)S(1)} %copy.17), channel_id=1, source_target_pairs={{0,1},{1,2},{2,3},{3,4},{4,5},{5,6},{6,7},{7,8},{8,9},{9,10},{10,1... | collective-permute-start | bytes 1216520 | tf_op jit(solution)/shard_map/ppermute | solution.py:17
  28.5 18.3 %collective-permute-start.3 = (bf16[3,22,3,1024]{3,1,2,0:T(8,128)(2,1)S(1)}, bf16[3,22,3,1024]{3,1,2,0:T(8,128)(2,1)S(1)}, u32[]{:S(2)}, u32[]{:S(2)}) collective-permute-start(bf16[3,22,3,1024]{3,1,2,0:T(8,128)(2,1)S(1)} %copy.18), channel_id=1, source_target_pairs={{1,0},{2,1},{3,2},{4,3},{5,4},{6,5},{7,6},{8,7},{9,8},{10,9},{11,1... | collective-permute-start | bytes 1216520 | tf_op jit(solution)/shard_map/ppermute | solution.py:18
  144.3 0.7 copy-start.5
  146.6 36.3 %copy-start.1 = (bf16[3,16,16,1024]{3,2,1,0:T(8,128)(2,1)S(1)}, bf16[3,16,16,1024]{3,2,1,0:T(8,128)(2,1)}, u32[]{:S(2)}) copy-start(bf16[3,16,16,1024]{3,2,1,0:T(8,128)(2,1)} %param.8) | copy-start | bytes 4718596
  146.6 36.3 %copy-start.7 = (f32[1024]{0:T(1024)S(1)}, f32[1024]{0:T(1024)}, u32[]{:S(2)}) copy-start(f32[1024]{0:T(1024)} %param.13) | copy-start | bytes 12292
  182.9 11.2 %copy-start.6 = (bf16[768]{0:T(1024)(128)(2,1)S(1)}, bf16[768]{0:T(1024)(128)(2,1)}, u32[]{:S(2)}) copy-start(bf16[768]{0:T(1024)(128)(2,1)} %convert_element_type.57) | copy-start | bytes 4612
  194.1 4.0 copy-start.3
  194.1 4.0 copy-start.4
Sparse Core Ops, SparseCore 0:
  9.7 67.4 all-gather.2
  79.0 63.3 all-gather.4
  199.7 270.3 all-reduce.4
where the time goes:
time: 483 us; the launch traced here: 479 us
  waiting for transfers between devices  290 us (60%)
  other arithmetic  103 us (21%)
  matrix products  52.9 us (11%)
  between operations  14 us (3%)
  starting transfers between devices  12.6 us (3%)
  local copies, waits for them, and re-layouts  7.07 us (1%)
    unnamed x4, waiting for transfers between devices  271 us
    reduce_sum x1, other arithmetic, apply_norm(): mean = jnp.mean(rows, axis=-1, keepdims=True)  92.9 us
    dot_general x1, matrix products, expand(): jnp.dot(normed, piece, preferred_element_type=jnp.float32)  36.3 us
    dot_general x1, matrix products, contract(): lax.dot_general(hidden, piece, (((1,), (1,)), ((), ())), preferred_elemen...  11.2 us
  transfers between devices with their start and end apart: 7, of which 4 were waited for; matrix products, arithmetic and copies ran while one was open for 30% of the time, Pallas kernels for 0%

commit v1 on v0

--- a/solution.py
+++ b/solution.py
@@ -39,6 +39,13 @@
     )
 
 
+def col_first(rows):
+    count, width = rows.shape
+    nrow, ncol = lax.axis_size("row"), lax.axis_size("col")
+    split = rows.reshape(count, nrow, ncol, width // (nrow * ncol))
+    return split.transpose(0, 2, 1, 3).reshape(count, width)
+
+
 def on_device(features, dw_kernel, ln_gain, w_in, w_down, gamma, labels, valid):
     tiles, high, wide, width = features.shape
     padded = with_halo(features, (("row", 1), ("col", 2)), 3).astype(jnp.float32)
@@ -58,15 +65,13 @@
     onehot = (labels.reshape(count, 1) == classes[None, :]).astype(jnp.float32)
     targets = ((onehot - 1.0 / NCLS) * keep.astype(jnp.float32)).astype(jnp.bfloat16)
     gram_part = lax.dot_general(
-        masked, out, (((0,), (0,)), ((), ())), preferred_element_type=jnp.float32
+        col_first(masked), out, (((0,), (0,)), ((), ())), preferred_element_type=jnp.float32
     )
     cross_part = lax.dot_general(
-        out, targets, (((0,), (0,)), ((), ())), preferred_element_type=jnp.float32
+        col_first(out), targets, (((0,), (0,)), ((), ())), preferred_element_type=jnp.float32
     )
-    gram_sum, cross_sum = (
-        lax.psum_scatter(gram_part, ("row", "col"), scatter_dimension=0, tiled=True),
-        lax.psum_scatter(cross_part, ("row", "col"), scatter_dimension=0, tiled=True),
-    )
+    parts = lax.psum_scatter((gram_part, cross_part), "col", scatter_dimension=0, tiled=True)
+    gram_sum, cross_sum = lax.psum_scatter(parts, "row", scatter_dimension=0, tiled=True)
     total = float(tiles * high * lax.axis_size("row") * wide * lax.axis_size("col"))
     return (gram_sum / total, cross_sum / jnp.sqrt(jnp.float32(total)))
 

time: 483 us -> 510 us (1.056)
  blocking collectives: 0 us -> 34.4 us
  waiting for transfers between devices: 290 us -> 268 us
  local copies, waits for them, and re-layouts: 7.07 us -> 14.3 us
    unnamed x4 -> x7, waiting for transfers between devices: 271 us -> 186 us
    reduce_scatter x0 -> x1, waiting for transfers between devices: none -> 61.7 us  [on_device(): lax.psum_scatter((gram_part, cross_part), 'col', scatter_dimension=0, til...]
    unnamed x0 -> x1, blocking collectives: none -> 34.4 us
  transfers between devices with their start and end apart: 7 -> 9, of which waited for: 4 -> 7; matrix products, arithmetic and copies ran while one was open for 30% -> 29% of each run, Pallas kernels for 0% -> 0%
where the time goes in v1:
time: 510 us; the launch traced here: 503 us
  waiting for transfers between devices  268 us (53%)
  other arithmetic  103 us (20%)
  matrix products  55.5 us (11%)
  blocking collectives  34.4 us (7%)
  between operations  14.7 us (3%)
  local copies, waits for them, and re-layouts  14.3 us (3%)
  starting transfers between devices  12.7 us (2%)
    unnamed x7, waiting for transfers between devices  186 us
    reduce_sum x1, other arithmetic, apply_norm(): mean = jnp.mean(rows, axis=-1, keepdims=True)  94 us
    reduce_scatter x1, waiting for transfers between devices, on_device(): lax.psum_scatter((gram_part, cross_part), 'col', scatter_dimension=0, til...  61.7 us
    dot_general x1, matrix products, expand(): jnp.dot(normed, piece, preferred_element_type=jnp.float32)  36.2 us
    unnamed x1, blocking collectives  34.4 us
    dot_general x1, matrix products, contract(): lax.dot_general(hidden, piece, (((1,), (1,)), ((), ())), preferred_elemen...  12.8 us
    ppermute x2, waiting for transfers between devices, with_halo(): before = lax.ppermute(last, axis, up)  10.9 us
  transfers between devices with their start and end apart: 9, of which 7 were waited for; matrix products, arithmetic and copies ran while one was open for 29% of the time, Pallas kernels for 0%

profile of v1, /device:TPU:120, one launch (start us, length us, event | category | flops | bytes accessed | tf_op | source)
XLA Modules:
  0.0 502.8 jit_solution(6221621563707724447)
XLA Ops:
  9.1 5.0 %collective-permute-start = (bf16[3,3,16,1024]{3,2,1,0:T(8,128)(2,1)S(1)}, bf16[3,3,16,1024]{3,2,1,0:T(8,128)(2,1)S(1)}, u32[]{:S(2)}, u32[]{:S(2)}) collective-permute-start(bf16[3,3,16,1024]{3,2,1,0:T(8,128)(2,1)S(1)} %get-tuple-element.17), channel_id=1, source_target_pairs={{0,16},{16,32},{32,48},{48,64},{64,80},{80,96},{96,112},{112,128},... | collective-permute-start | bytes 884744 | tf_op jit(solution)/shard_map/ppermute | solution.py:17
  14.1 1.9 collective-permute-start.1
  16.1 1.2 fusion.105
  17.3 1.4 fusion.108
  18.8 1.6 collective-permute-done
  20.6 5.1 %collective-permute-done.1 = bf16[3,3,16,1024]{3,2,1,0:T(8,128)(2,1)S(1)} collective-permute-done((bf16[3,3,16,1024]{3,2,1,0:T(8,128)(2,1)S(1)}, bf16[3,3,16,1024]{3,2,1,0:T(8,128)(2,1)S(1)}, u32[]{:S(2)}, u32[]{:S(2)}) %collective-permute-start.1) | collective-permute-done | bytes 294944 | tf_op jit(solution)/shard_map/ppermute | solution.py:18
  26.4 1.9 collective-permute-start.2
  28.4 3.6 collective-permute-start.3
  32.2 9.4 %collective-permute-done.2 = bf16[3,22,3,1024]{3,1,2,0:T(8,128)(2,1)S(1)} collective-permute-done((bf16[3,22,3,1024]{3,1,2,0:T(8,128)(2,1)S(1)}, bf16[3,22,3,1024]{3,1,2,0:T(8,128)(2,1)S(1)}, u32[]{:S(2)}, u32[]{:S(2)}) %collective-permute-start.2) | collective-permute-done | bytes 405536 | tf_op jit(solution)/shard_map/ppermute | solution.py:17
  41.9 4.8 collective-permute-done.3
  47.1 4.3 maximum_convert_fusion
  51.4 94.0 %fusion.101 = (f32[3,16,16]{2,1,0:T(8,128)S(1)}, f32[3,16,16,1024]{3,2,1,0:T(8,128)S(1)}) fusion(f32[1024]{0:T(1024)S(1)} %bitcast.119, f32[3,22,22,1024]{3,2,1,0:T(8,128)} %maximum_convert_fusion, f32[1024]{0:T(1024)S(1)} %bitcast.118, f32[1024]{0:T(1024)S(1)} %bitcast.117, f32[1024]{0:T(1024)S(1)} %bitcast.116, f32[1024]{0:T(1024)S(1)} %bitcast.115, ...), kind=kLoop, calls=%fused_computation.170 | loop fusion | flops 77069568 | bytes 157490176 | tf_op jit(solution)/shard_map/reduce_sum | solution.py:24
  146.1 1.6 fusion.63
  147.7 36.2 %fusion.65.clone.4 = bf16[768,4096]{1,0:T(8,128)(2,1)} fusion(bf16[768,1024]{1,0:T(8,128)(2,1)} %fusion.63, bf16[1024,4096]{1,0:T(8,128)(2,1)} %all-gather.3.cloned.1.call-done), kind=kOutput, calls=%fused_computation.3.clone.clone.clone.clone.clone.clone.1 | convolution fusion | flops 6646923264 | bytes 16252928 | tf_op jit(solution)/shard_map/dot_general | solution.py:32
  183.9 12.8 %broadcast_multiply_fusion = (bf16[768,1024]{1,0:T(8,128)(2,1)}, bf16[768,1024]{1,0:T(8,128)(2,1)}) fusion(bf16[768]{0:T(1024)(128)(2,1)S(1)} %convert_element_type.57, bf16[1024,4096]{1,0:T(8,128)(2,1)} %all-gather.5.cloned.1.call-done, f32[1024]{0:T(1024)S(1)} %copy-done.7, bf16[768,1024]{1,0:T(8,128)(2,1)S(1)} %bitcast.89, ...), kind=kOutput, calls=%fused_computation.125 | convolution fusion | flops 6446383104 | bytes 19404288 | tf_op jit(solution)/shard_map/dot_general | solution.py:37
  196.7 1.7 copy.37
  199.6 1.4 reshape.126
  201.5 5.2 %fusion.111 = f32[1024,1024]{1,0:T(8,128)} fusion(bf16[768,1024]{0,1:T(8,128)(2,1)} %reshape.126, bf16[768,1024]{1,0:T(8,128)(2,1)S(1)} %copy-done.2), kind=kOutput, calls=%fused_computation.178 | convolution fusion | flops 1610612736 | bytes 7340032 | tf_op jit(solution)/shard_map/dot_general | solution.py:67
  209.8 1.4 fusion.66
  211.3 61.7 %reduce-scatter.6.cloned.1.call-done = f32[64,1024]{1,0:T(8,128)} async-done(((f32[1024,1024]{1,0:T(8,128)}), f32[64,1024]{1,0:T(8,128)}) %reduce-scatter.6.cloned.1.call-update) | async-done | bytes 262160 | tf_op jit(solution)/shard_map/reduce_scatter | solution.py:73
  274.2 63.9 %reduce-scatter.8.cloned.1.call-done = f32[64,16]{1,0:T(8,128)} async-done(((f32[1024,16]{1,0:T(8,128)}), f32[64,16]{1,0:T(8,128)}) %reduce-scatter.8.cloned.1.call-update) | async-done | bytes 4112
  339.0 34.4 %all-reduce.1 = f32[64,16]{0,1:T(8,128)S(1)} all-reduce(f32[64,16]{0,1:T(8,128)S(1)} %copy.43), channel_id=5, replica_groups=mesh['row'=16,'col'=16] {'row'}, use_global_device_ids=true, to_apply=%region_5.0.clone | all-reduce | flops 1024 | bytes 8192
  374.1 120.8 %all-reduce.4.cloned.1.call-done = f32[64,1024]{1,0:T(8,128)} async-done(((f32[64,1024]{1,0:T(8,128)}), f32[64,1024]{1,0:T(8,128)}) %all-reduce.4.cloned.1.call-update) | async-done | bytes 262160
  494.9 1.4 dynamic-slice_multiply_fusion
  (59 shorter events, 11.5 us)
Async XLA Ops:
  7.2 13.2 %copy-start = (bf16[3,16,16,1024]{3,2,1,0:T(8,128)(2,1)S(1)}, bf16[3,16,16,1024]{3,2,1,0:T(8,128)(2,1)}, u32[]{:S(2)}) copy-start(bf16[3,16,16,1024]{3,2,1,0:T(8,128)(2,1)} %param.8) | copy-start | bytes 4718596
  7.2 140.5 %all-gather.3.cloned.1.call-start = ((), (), s32[]{:S(2)}) async-start(), calls=%async_computation.2 | async-start | bytes 8912896 | tf_op jit(solution)/shard_map/all_gather | solution.py:59
  7.9 176.0 %all-gather.5.cloned.1.call-start = ((), (), s32[]{:S(2)}) async-start(), calls=%async_computation.3 | async-start | bytes 8912896 | tf_op jit(solution)/shard_map/all_gather | solution.py:60
  9.1 11.3 %collective-permute-start = (bf16[3,3,16,1024]{3,2,1,0:T(8,128)(2,1)S(1)}, bf16[3,3,16,1024]{3,2,1,0:T(8,128)(2,1)S(1)}, u32[]{:S(2)}, u32[]{:S(2)}) collective-permute-start(bf16[3,3,16,1024]{3,2,1,0:T(8,128)(2,1)S(1)} %get-tuple-element.17), channel_id=1, source_target_pairs={{0,16},{16,32},{32,48},{48,64},{64,80},{80,96},{96,112},{112,128},... | collective-permute-start | bytes 884744 | tf_op jit(solution)/shard_map/ppermute | solution.py:17
  14.1 11.6 %collective-permute-start.1 = (bf16[3,3,16,1024]{3,2,1,0:T(8,128)(2,1)S(1)}, bf16[3,3,16,1024]{3,2,1,0:T(8,128)(2,1)S(1)}, u32[]{:S(2)}, u32[]{:S(2)}) collective-permute-start(bf16[3,3,16,1024]{3,2,1,0:T(8,128)(2,1)S(1)} %get-tuple-element.16), channel_id=1, source_target_pairs={{16,0},{32,16},{48,32},{64,48},{80,64},{96,80},{112,96},{128,112},... | collective-permute-start | bytes 884744 | tf_op jit(solution)/shard_map/ppermute | solution.py:18
  16.1 256.9 %reduce-scatter.6.cloned.1.call-start = ((), (), s32[]{:S(2)}) async-start(), calls=%async_computation.4 | async-start | bytes 4456448 | tf_op jit(solution)/shard_map/reduce_scatter | solution.py:73
  20.6 11.5 %copy-start.3 = (bf16[7,7,1024]{2,1,0:T(8,128)(2,1)S(1)}, bf16[7,7,1024]{2,1,0:T(8,128)(2,1)}, u32[]{:S(2)}) copy-start(bf16[7,7,1024]{2,1,0:T(8,128)(2,1)} %param.9) | copy-start | bytes 301060
  26.4 15.2 %collective-permute-start.2 = (bf16[3,22,3,1024]{3,1,2,0:T(8,128)(2,1)S(1)}, bf16[3,22,3,1024]{3,1,2,0:T(8,128)(2,1)S(1)}, u32[]{:S(2)}, u32[]{:S(2)}) collective-permute-start(bf16[3,22,3,1024]{3,1,2,0:T(8,128)(2,1)S(1)} %copy.33), channel_id=1, source_target_pairs={{0,1},{1,2},{2,3},{3,4},{4,5},{5,6},{6,7},{7,8},{8,9},{9,10},{10,1... | collective-permute-start | bytes 1216520 | tf_op jit(solution)/shard_map/ppermute | solution.py:17
  28.4 18.3 %collective-permute-start.3 = (bf16[3,22,3,1024]{3,1,2,0:T(8,128)(2,1)S(1)}, bf16[3,22,3,1024]{3,1,2,0:T(8,128)(2,1)S(1)}, u32[]{:S(2)}, u32[]{:S(2)}) collective-permute-start(bf16[3,22,3,1024]{3,1,2,0:T(8,128)(2,1)S(1)} %copy.34), channel_id=1, source_target_pairs={{1,0},{2,1},{3,2},{4,3},{5,4},{6,5},{7,6},{8,7},{9,8},{10,9},{11,1... | collective-permute-start | bytes 1216520 | tf_op jit(solution)/shard_map/ppermute | solution.py:18
  145.4 0.7 copy-start.6
  147.7 36.3 %copy-start.1 = (bf16[3,16,16,1024]{3,2,1,0:T(8,128)(2,1)S(1)}, bf16[3,16,16,1024]{3,2,1,0:T(8,128)(2,1)}, u32[]{:S(2)}) copy-start(bf16[3,16,16,1024]{3,2,1,0:T(8,128)(2,1)} %param.8) | copy-start | bytes 4718596
  147.7 36.3 %copy-start.7 = (f32[1024]{0:T(1024)S(1)}, f32[1024]{0:T(1024)}, u32[]{:S(2)}) copy-start(f32[1024]{0:T(1024)} %param.13) | copy-start | bytes 12292
  199.6 2.0 copy-start.2
  206.7 0.7 copy-start.4
  206.7 0.8 copy-start.5
  206.7 131.4 %reduce-scatter.8.cloned.1.call-start = ((), (), s32[]{:S(2)}) async-start(), calls=%async_computation.5 | async-start | bytes 557056
  209.4 63.6 %copy-start.8 = (u32[256]{0:T(256)S(1)}, u32[256]{0:T(256)}, u32[]{:S(2)}) copy-start(u32[256]{0:T(256)} %constant.78) | copy-start | bytes 3076
  211.2 283.7 %all-reduce.4.cloned.1.call-start = ((), (), s32[]{:S(2)}) async-start(), calls=%async_computation.6 | async-start | bytes 524288
Sparse Core Ops, SparseCore 0:
  9.7 67.4 all-gather.2
  79.0 63.4 all-gather.4
  206.8 66.0 reduce-scatter.5
  275.3 62.7 reduce-scatter.7
  340.6 154.2 all-reduce.3

commit v2 on v0

--- a/solution.py
+++ b/solution.py
@@ -39,6 +39,38 @@
     )
 
 
+HALVING_BITS = (0, 1, 3, 4, 2, 5, 7, 6)
+
+
+def halving_order(rows):
+    count, width = rows.shape
+    nbits = len(HALVING_BITS)
+    split = rows.reshape((count,) + (2,) * nbits + (width >> nbits,))
+    order = (0,) + tuple(nbits - bit for bit in HALVING_BITS) + (nbits + 1,)
+    return split.transpose(order).reshape(count, width)
+
+
+def halving_sum(part, axes):
+    size = 1
+    for axis in axes:
+        size *= lax.axis_size(axis)
+    me = lax.axis_index(axes)
+    for bit in HALVING_BITS:
+        mine = (me >> bit) & 1
+        halves = part.reshape((2, part.shape[0] // 2) + part.shape[1:])
+        keep = lax.dynamic_index_in_dim(halves, mine, 0, keepdims=False)
+        send = lax.dynamic_index_in_dim(halves, 1 - mine, 0, keepdims=False)
+        pairs = [(i, i ^ (1 << bit)) for i in range(size)]
+        part = keep + lax.ppermute(send, axes, pairs)
+    return part
+
+
+def targets_of(labels, count):
+    classes = jnp.arange(NCLS, dtype=jnp.int32)
+    onehot = (labels.reshape(count, 1) == classes[None, :]).astype(jnp.float32)
+    return (onehot - 1.0 / NCLS).astype(jnp.bfloat16)
+
+
 def on_device(features, dw_kernel, ln_gain, w_in, w_down, gamma, labels, valid):
     tiles, high, wide, width = features.shape
     padded = with_halo(features, (("row", 1), ("col", 2)), 3).astype(jnp.float32)
@@ -54,19 +86,14 @@
     out = (features.reshape(count, width).astype(jnp.float32) + gamma * branch).astype(jnp.bfloat16)
     keep = valid.reshape(count, 1)
     masked = out * keep.astype(jnp.bfloat16)
-    classes = jnp.arange(NCLS, dtype=jnp.int32)
-    onehot = (labels.reshape(count, 1) == classes[None, :]).astype(jnp.float32)
-    targets = ((onehot - 1.0 / NCLS) * keep.astype(jnp.float32)).astype(jnp.bfloat16)
-    gram_part = lax.dot_general(
-        masked, out, (((0,), (0,)), ((), ())), preferred_element_type=jnp.float32
+    both = lax.dot_general(
+        halving_order(masked),
+        jnp.concatenate([out, targets_of(labels, count)], axis=1),
+        (((0,), (0,)), ((), ())),
+        preferred_element_type=jnp.float32,
     )
-    cross_part = lax.dot_general(
-        out, targets, (((0,), (0,)), ((), ())), preferred_element_type=jnp.float32
-    )
-    gram_sum, cross_sum = (
-        lax.psum_scatter(gram_part, ("row", "col"), scatter_dimension=0, tiled=True),
-        lax.psum_scatter(cross_part, ("row", "col"), scatter_dimension=0, tiled=True),
-    )
+    summed = halving_sum(both, ("row", "col"))
+    gram_sum, cross_sum = summed[:, :width], summed[:, width:]
     total = float(tiles * high * lax.axis_size("row") * wide * lax.axis_size("col"))
     return (gram_sum / total, cross_sum / jnp.sqrt(jnp.float32(total)))
 

time: 483 us -> 307 us (0.64)
  waiting for transfers between devices: 290 us -> 88.7 us
  local copies, waits for them, and re-layouts: 7.07 us -> 20.7 us
  starting transfers between devices: 12.6 us -> 22 us
  other arithmetic: 103 us -> 108 us
    unnamed x4 -> x2, waiting for transfers between devices: 271 us -> 0.7 us
    ppermute x0 -> x8, waiting for transfers between devices: none -> 68.1 us  [halving_sum(): part = keep + lax.ppermute(send, axes, pairs)]
    ppermute x0 -> x8, starting transfers between devices: none -> 9.39 us  [halving_sum(): part = keep + lax.ppermute(send, axes, pairs)]
  transfers between devices with their start and end apart: 7 -> 14, of which waited for: 4 -> 12; matrix products, arithmetic and copies ran while one was open for 30% -> 48% of each run, Pallas kernels for 0% -> 0%
where the time goes in v2:
time: 307 us; the launch traced here: 306 us
  other arithmetic  108 us (35%)
  waiting for transfers between devices  88.7 us (29%)
  matrix products  52.4 us (17%)
  starting transfers between devices  22 us (7%)
  local copies, waits for them, and re-layouts  20.7 us (7%)
  between operations  14.5 us (5%)
    reduce_sum x1, other arithmetic, apply_norm(): mean = jnp.mean(rows, axis=-1, keepdims=True)  95.9 us
    ppermute x8, waiting for transfers between devices, halving_sum(): part = keep + lax.ppermute(send, axes, pairs)  68.1 us
    dot_general x1, matrix products, expand(): jnp.dot(normed, piece, preferred_element_type=jnp.float32)  36.3 us
    dot_general x1, matrix products, contract(): lax.dot_general(hidden, piece, (((1,), (1,)), ((), ())), preferred_elemen...  12.8 us
    ppermute x2, waiting for transfers between devices, with_halo(): before = lax.ppermute(last, axis, up)  9.99 us
    ppermute x2, waiting for transfers between devices, with_halo(): after = lax.ppermute(leading, axis, down)  9.92 us
    ppermute x8, starting transfers between devices, halving_sum(): part = keep + lax.ppermute(send, axes, pairs)  9.39 us
    ppermute x2, starting transfers between devices, with_halo(): before = lax.ppermute(last, axis, up)  6.96 us
  transfers between devices with their start and end apart: 14, of which 12 were waited for; matrix products, arithmetic and copies ran while one was open for 48% of the time, Pallas kernels for 0%

profile of v2, /device:TPU:120, one launch (start us, length us, event | category | flops | bytes accessed | tf_op | source)
XLA Modules:
  0.0 306.1 jit_solution(11954538254147887759)
XLA Ops:
  9.1 5.0 %collective-permute-start = (bf16[3,3,16,1024]{3,2,1,0:T(8,128)(2,1)S(1)}, bf16[3,3,16,1024]{3,2,1,0:T(8,128)(2,1)S(1)}, u32[]{:S(2)}, u32[]{:S(2)}) collective-permute-start(bf16[3,3,16,1024]{3,2,1,0:T(8,128)(2,1)S(1)} %get-tuple-element.9), channel_id=1, source_target_pairs={{0,16},{16,32},{32,48},{48,64},{64,80},{80,96},{96,112},{112,128},... | collective-permute-start | bytes 884744 | tf_op jit(solution)/shard_map/ppermute | solution.py:17
  20.6 5.1 %collective-permute-done.1 = bf16[3,3,16,1024]{3,2,1,0:T(8,128)(2,1)S(1)} collective-permute-done((bf16[3,3,16,1024]{3,2,1,0:T(8,128)(2,1)S(1)}, bf16[3,3,16,1024]{3,2,1,0:T(8,128)(2,1)S(1)}, u32[]{:S(2)}, u32[]{:S(2)}) %collective-permute-start.1) | collective-permute-done | bytes 294944 | tf_op jit(solution)/shard_map/ppermute | solution.py:18
  28.4 3.6 %collective-permute-start.3 = (bf16[3,22,3,1024]{3,1,2,0:T(8,128)(2,1)S(1)}, bf16[3,22,3,1024]{3,1,2,0:T(8,128)(2,1)S(1)}, u32[]{:S(2)}, u32[]{:S(2)}) collective-permute-start(bf16[3,22,3,1024]{3,1,2,0:T(8,128)(2,1)S(1)} %copy.42), channel_id=1, source_target_pairs={{1,0},{2,1},{3,2},{4,3},{5,4},{6,5},{7,6},{8,7},{9,8},{10,9},{11,1... | collective-permute-start | bytes 1216520 | tf_op jit(solution)/shard_map/ppermute | solution.py:18
  32.2 9.4 %collective-permute-done.2 = bf16[3,22,3,1024]{3,1,2,0:T(8,128)(2,1)S(1)} collective-permute-done((bf16[3,22,3,1024]{3,1,2,0:T(8,128)(2,1)S(1)}, bf16[3,22,3,1024]{3,1,2,0:T(8,128)(2,1)S(1)}, u32[]{:S(2)}, u32[]{:S(2)}) %collective-permute-start.2) | collective-permute-done | bytes 405536 | tf_op jit(solution)/shard_map/ppermute | solution.py:17
  41.9 4.8 %collective-permute-done.3 = bf16[3,22,3,1024]{3,1,2,0:T(8,128)(2,1)S(1)} collective-permute-done((bf16[3,22,3,1024]{3,1,2,0:T(8,128)(2,1)S(1)}, bf16[3,22,3,1024]{3,1,2,0:T(8,128)(2,1)S(1)}, u32[]{:S(2)}, u32[]{:S(2)}) %collective-permute-start.3) | collective-permute-done | bytes 405536 | tf_op jit(solution)/shard_map/ppermute | solution.py:18
  47.1 4.3 %maximum_convert_fusion = f32[3,22,22,1024]{3,2,1,0:T(8,128)} fusion(bf16[3,22,3,1024]{3,2,1,0:T(4,128)(2,1)S(1)} %copy.44, bf16[3,22,16,1024]{3,2,1,0:T(8,128)(2,1)S(1)} %constant_dynamic-update-slice_fusion, bf16[3,22,3,1024]{3,2,1,0:T(4,128)(2,1)S(1)} %copy.43), kind=kLoop, calls=%fused_computation.20 | loop fusion | flops 8921088 | bytes 8921088 | tf_op jit(solution)/shard_map/convert_element_type | solution.py:76
  51.4 95.9 %fusion.101 = (f32[3,16,16]{2,1,0:T(8,128)S(1)}, f32[3,16,16,1024]{3,2,1,0:T(8,128)S(1)}) fusion(f32[1024]{0:T(1024)S(1)} %bitcast.165, f32[3,22,22,1024]{3,2,1,0:T(8,128)} %maximum_convert_fusion, f32[1024]{0:T(1024)S(1)} %bitcast.164, f32[1024]{0:T(1024)S(1)} %bitcast.163, f32[1024]{0:T(1024)S(1)} %bitcast.162, f32[1024]{0:T(1024)S(1)} %bitcast.161, ...), kind=kLoop, calls=%fused_computation.190 | loop fusion | flops 77069568 | bytes 157490176 | tf_op jit(solution)/shard_map/reduce_sum | solution.py:24
  149.6 36.3 %fusion.65.clone.4 = bf16[768,4096]{1,0:T(8,128)(2,1)} fusion(bf16[768,1024]{1,0:T(8,128)(2,1)} %fusion.63, bf16[1024,4096]{1,0:T(8,128)(2,1)} %all-gather.3.cloned.1.call-done), kind=kOutput, calls=%fused_computation.3.clone.clone.clone.clone.clone.clone.1 | convolution fusion | flops 6646923264 | bytes 16252928 | tf_op jit(solution)/shard_map/dot_general | solution.py:32
  185.9 12.8 %broadcast_multiply_fusion = (bf16[768,1024]{1,0:T(8,128)(2,1)}, bf16[768,1024]{1,0:T(8,128)(2,1)}) fusion(bf16[768]{0:T(1024)(128)(2,1)S(1)} %convert_element_type.46, bf16[1024,4096]{1,0:T(8,128)(2,1)} %all-gather.5.cloned.1.call-done, f32[1024]{0:T(1024)S(1)} %copy-done.6, bf16[768,1024]{1,0:T(8,128)(2,1)S(1)} %bitcast.126, ...), kind=kOutput, calls=%fused_computation.133 | convolution fusion | flops 6446383104 | bytes 19404288 | tf_op jit(solution)/shard_map/dot_general | solution.py:37
  202.1 3.3 %fusion.66 = f32[2,512,1040]{1,2,0:T(8,128)S(1)} fusion(bf16[2,512,768]{2,1,0:T(8,128)(2,1)S(1)} %bitcast.129, bf16[768,16]{1,0:T(8,128)(2,1)S(1)} %copy-done.4, bf16[768,1024]{1,0:T(8,128)(2,1)} %get-tuple-element.62), kind=kOutput, calls=%fused_computation.128 | convolution fusion | flops 1638973440 | bytes 7430144 | tf_op jit(solution)/shard_map/dot_general | solution.py:89
  205.4 2.0 copy-done
  208.9 4.4 %collective-permute-done.4 = f32[512,1040]{0,1:T(8,128)S(1)} collective-permute-done((f32[512,1040]{0,1:T(8,128)}, f32[512,1040]{0,1:T(8,128)S(1)}, u32[]{:S(2)}, u32[]{:S(2)}) %collective-permute-start.4) | collective-permute-done | bytes 2129952 | tf_op jit(solution)/shard_map/ppermute | solution.py:64
  213.4 3.5 %bitcast_add_fusion = f32[512,1040]{0,1:T(8,128)} fusion(f32[512,1040]{0,1:T(8,128)S(1)} %collective-permute-done.4, f32[2,512,1040]{1,2,0:T(8,128)} %copy-done, s32[]{:T(128)S(6)} %select_n.56), kind=kLoop, calls=%fused_computation.125 | loop fusion | flops 532480 | bytes 6389764 | tf_op jit(solution)/shard_map/add | solution.py:64
  216.8 2.7 reshape.136
  221.5 2.4 collective-permute-start.5
  223.9 24.0 %collective-permute-done.5 = f32[256,1040]{0,1:T(8,128)S(1)} collective-permute-done((f32[256,1040]{0,1:T(8,128)S(1)}, f32[256,1040]{0,1:T(8,128)S(1)}, u32[]{:S(2)}, u32[]{:S(2)}) %collective-permute-start.5) | collective-permute-done | bytes 1064992 | tf_op jit(solution)/shard_map/ppermute | solution.py:64
  251.0 12.7 %collective-permute-done.6 = f32[128,1040]{0,1:T(8,128)S(1)} collective-permute-done((f32[128,1040]{0,1:T(8,128)S(1)}, f32[128,1040]{0,1:T(8,128)S(1)}, u32[]{:S(2)}, u32[]{:S(2)}) %collective-permute-start.6) | collective-permute-done | bytes 532512 | tf_op jit(solution)/shard_map/ppermute | solution.py:64
  264.2 7.8 %collective-permute-done.7 = f32[64,1040]{1,0:T(8,128)S(1)} collective-permute-done((f32[64,1040]{1,0:T(8,128)S(1)}, f32[64,1040]{1,0:T(8,128)S(1)}, u32[]{:S(2)}, u32[]{:S(2)}) %collective-permute-start.7) | collective-permute-done | bytes 266272 | tf_op jit(solution)/shard_map/ppermute | solution.py:64
  272.2 6.6 %collective-permute-done.8 = f32[32,1040]{1,0:T(8,128)S(1)} collective-permute-done((f32[32,1040]{1,0:T(8,128)S(1)}, f32[32,1040]{1,0:T(8,128)S(1)}, u32[]{:S(2)}, u32[]{:S(2)}) %collective-permute-start.8) | collective-permute-done | bytes 133152 | tf_op jit(solution)/shard_map/ppermute | solution.py:64
  278.9 5.7 %collective-permute-done.9 = f32[16,1040]{1,0:T(8,128)S(1)} collective-permute-done((f32[16,1040]{1,0:T(8,128)S(1)}, f32[16,1040]{1,0:T(8,128)S(1)}, u32[]{:S(2)}, u32[]{:S(2)}) %collective-permute-start.9) | collective-permute-done | bytes 66592 | tf_op jit(solution)/shard_map/ppermute | solution.py:64
  284.7 2.8 collective-permute-start.10
  287.5 2.7 collective-permute-done.10
  290.3 3.8 %collective-permute-start.11 = (f32[4,1040]{1,0:T(4,128)S(1)}, f32[4,1040]{1,0:T(4,128)S(1)}, u32[]{:S(2)}, u32[]{:S(2)}) collective-permute-start(f32[4,1040]{1,0:T(4,128)S(1)} %dynamic-slice_bitcast_fusion.5), channel_id=1, source_target_pairs={{0,64},{1,65},{2,66},{3,67},{4,68},{5,69},{6,70},{7,71},{8,72},{9,... | collective-permute-start | bytes 49928 | tf_op jit(solution)/shard_map/ppermute | solution.py:64
  294.1 4.0 %collective-permute-done.11 = f32[4,1040]{1,0:T(4,128)S(1)} collective-permute-done((f32[4,1040]{1,0:T(4,128)S(1)}, f32[4,1040]{1,0:T(4,128)S(1)}, u32[]{:S(2)}, u32[]{:S(2)}) %collective-permute-start.11) | collective-permute-done | bytes 16672 | tf_op jit(solution)/shard_map/ppermute | solution.py:64
  (76 shorter events, 25.9 us)
Async XLA Ops:
  7.2 13.2 %copy-start.1 = (bf16[3,16,16,1024]{3,2,1,0:T(8,128)(2,1)S(1)}, bf16[3,16,16,1024]{3,2,1,0:T(8,128)(2,1)}, u32[]{:S(2)}) copy-start(bf16[3,16,16,1024]{3,2,1,0:T(8,128)(2,1)} %param.8) | copy-start | bytes 4718596
  7.2 142.5 %all-gather.3.cloned.1.call-start = ((), (), s32[]{:S(2)}) async-start(), calls=%async_computation | async-start | bytes 8912896 | tf_op jit(solution)/shard_map/all_gather | solution.py:84
  7.9 178.0 %all-gather.5.cloned.1.call-start = ((), (), s32[]{:S(2)}) async-start(), calls=%async_computation.1 | async-start | bytes 8912896 | tf_op jit(solution)/shard_map/all_gather | solution.py:85
  9.1 11.3 %collective-permute-start = (bf16[3,3,16,1024]{3,2,1,0:T(8,128)(2,1)S(1)}, bf16[3,3,16,1024]{3,2,1,0:T(8,128)(2,1)S(1)}, u32[]{:S(2)}, u32[]{:S(2)}) collective-permute-start(bf16[3,3,16,1024]{3,2,1,0:T(8,128)(2,1)S(1)} %get-tuple-element.9), channel_id=1, source_target_pairs={{0,16},{16,32},{32,48},{48,64},{64,80},{80,96},{96,112},{112,128},... | collective-permute-start | bytes 884744 | tf_op jit(solution)/shard_map/ppermute | solution.py:17
  14.1 11.6 %collective-permute-start.1 = (bf16[3,3,16,1024]{3,2,1,0:T(8,128)(2,1)S(1)}, bf16[3,3,16,1024]{3,2,1,0:T(8,128)(2,1)S(1)}, u32[]{:S(2)}, u32[]{:S(2)}) collective-permute-start(bf16[3,3,16,1024]{3,2,1,0:T(8,128)(2,1)S(1)} %get-tuple-element.8), channel_id=1, source_target_pairs={{16,0},{32,16},{48,32},{64,48},{80,64},{96,80},{112,96},{128,112},... | collective-permute-start | bytes 884744 | tf_op jit(solution)/shard_map/ppermute | solution.py:18
  20.6 11.5 %copy-start.3 = (bf16[7,7,1024]{2,1,0:T(8,128)(2,1)S(1)}, bf16[7,7,1024]{2,1,0:T(8,128)(2,1)}, u32[]{:S(2)}) copy-start(bf16[7,7,1024]{2,1,0:T(8,128)(2,1)} %param.9) | copy-start | bytes 301060
  26.4 15.2 %collective-permute-start.2 = (bf16[3,22,3,1024]{3,1,2,0:T(8,128)(2,1)S(1)}, bf16[3,22,3,1024]{3,1,2,0:T(8,128)(2,1)S(1)}, u32[]{:S(2)}, u32[]{:S(2)}) collective-permute-start(bf16[3,22,3,1024]{3,1,2,0:T(8,128)(2,1)S(1)} %copy.41), channel_id=1, source_target_pairs={{0,1},{1,2},{2,3},{3,4},{4,5},{5,6},{6,7},{7,8},{8,9},{9,10},{10,1... | collective-permute-start | bytes 1216520 | tf_op jit(solution)/shard_map/ppermute | solution.py:17
  28.4 18.3 %collective-permute-start.3 = (bf16[3,22,3,1024]{3,1,2,0:T(8,128)(2,1)S(1)}, bf16[3,22,3,1024]{3,1,2,0:T(8,128)(2,1)S(1)}, u32[]{:S(2)}, u32[]{:S(2)}) collective-permute-start(bf16[3,22,3,1024]{3,1,2,0:T(8,128)(2,1)S(1)} %copy.42), channel_id=1, source_target_pairs={{1,0},{2,1},{3,2},{4,3},{5,4},{6,5},{7,6},{8,7},{9,8},{10,9},{11,1... | collective-permute-start | bytes 1216520 | tf_op jit(solution)/shard_map/ppermute | solution.py:18
  147.3 0.7 copy-start.5
  149.6 36.3 %copy-start.2 = (bf16[3,16,16,1024]{3,2,1,0:T(8,128)(2,1)S(1)}, bf16[3,16,16,1024]{3,2,1,0:T(8,128)(2,1)}, u32[]{:S(2)}) copy-start(bf16[3,16,16,1024]{3,2,1,0:T(8,128)(2,1)} %param.8) | copy-start | bytes 4718596
  149.6 36.3 %copy-start.6 = (f32[1024]{0:T(1024)S(1)}, f32[1024]{0:T(1024)}, u32[]{:S(2)}) copy-start(f32[1024]{0:T(1024)} %param.13) | copy-start | bytes 12292
  200.8 1.2 copy-start.4
  205.4 2.0 copy-start
  208.9 4.4 %collective-permute-start.4 = (f32[512,1040]{0,1:T(8,128)}, f32[512,1040]{0,1:T(8,128)S(1)}, u32[]{:S(2)}, u32[]{:S(2)}) collective-permute-start(f32[512,1040]{0,1:T(8,128)} %dynamic-slice_bitcast_fusion), channel_id=1, source_target_pairs={{0,1},{1,0},{2,3},{3,2},{4,5},{5,4},{6,7},{7,6},{8,9},{9,8},{10,11... | collective-permute-start | bytes 6389768 | tf_op jit(solution)/shard_map/ppermute | solution.py:64
  221.5 26.5 %collective-permute-start.5 = (f32[256,1040]{0,1:T(8,128)S(1)}, f32[256,1040]{0,1:T(8,128)S(1)}, u32[]{:S(2)}, u32[]{:S(2)}) collective-permute-start(f32[256,1040]{0,1:T(8,128)S(1)} %bitcast.132), channel_id=1, source_target_pairs={{0,2},{1,3},{2,0},{3,1},{4,6},{5,7},{6,4},{7,5},{8,10},{9,11},{10,... | collective-permute-start | bytes 3194888 | tf_op jit(solution)/shard_map/ppermute | solution.py:64
  249.8 13.9 %collective-permute-start.6 = (f32[128,1040]{0,1:T(8,128)S(1)}, f32[128,1040]{0,1:T(8,128)S(1)}, u32[]{:S(2)}, u32[]{:S(2)}) collective-permute-start(f32[128,1040]{0,1:T(8,128)S(1)} %bitcast.135), channel_id=1, source_target_pairs={{0,8},{1,9},{2,10},{3,11},{4,12},{5,13},{6,14},{7,15},{8,0},{9,1},... | collective-permute-start | bytes 1597448 | tf_op jit(solution)/shard_map/ppermute | solution.py:64
  264.0 7.9 %collective-permute-start.7 = (f32[64,1040]{1,0:T(8,128)S(1)}, f32[64,1040]{1,0:T(8,128)S(1)}, u32[]{:S(2)}, u32[]{:S(2)}) collective-permute-start(f32[64,1040]{1,0:T(8,128)S(1)} %dynamic-slice_bitcast_fusion.1), channel_id=1, source_target_pairs={{0,16},{1,17},{2,18},{3,19},{4,20},{5,21},{6,22},{7,23},{8,24},{9,... | collective-permute-start | bytes 798728 | tf_op jit(solution)/shard_map/ppermute | solution.py:64
  272.1 6.7 %collective-permute-start.8 = (f32[32,1040]{1,0:T(8,128)S(1)}, f32[32,1040]{1,0:T(8,128)S(1)}, u32[]{:S(2)}, u32[]{:S(2)}) collective-permute-start(f32[32,1040]{1,0:T(8,128)S(1)} %dynamic-slice_bitcast_fusion.2), channel_id=1, source_target_pairs={{0,4},{1,5},{2,6},{3,7},{4,0},{5,1},{6,2},{7,3},{8,12},{9,13},{10,... | collective-permute-start | bytes 399368 | tf_op jit(solution)/shard_map/ppermute | solution.py:64
  278.8 5.9 %collective-permute-start.9 = (f32[16,1040]{1,0:T(8,128)S(1)}, f32[16,1040]{1,0:T(8,128)S(1)}, u32[]{:S(2)}, u32[]{:S(2)}) collective-permute-start(f32[16,1040]{1,0:T(8,128)S(1)} %dynamic-slice_bitcast_fusion.3), channel_id=1, source_target_pairs={{0,32},{1,33},{2,34},{3,35},{4,36},{5,37},{6,38},{7,39},{8,40},{9,... | collective-permute-start | bytes 199688 | tf_op jit(solution)/shard_map/ppermute | solution.py:64
  284.7 5.5 %collective-permute-start.10 = (f32[8,1040]{1,0:T(8,128)S(1)}, f32[8,1040]{1,0:T(8,128)S(1)}, u32[]{:S(2)}, u32[]{:S(2)}) collective-permute-start(f32[8,1040]{1,0:T(8,128)S(1)} %dynamic-slice_bitcast_fusion.4), channel_id=1, source_target_pairs={{0,128},{1,129},{2,130},{3,131},{4,132},{5,133},{6,134},{7,135},{8... | collective-permute-start | bytes 99848 | tf_op jit(solution)/shard_map/ppermute | solution.py:64
  290.3 7.8 %collective-permute-start.11 = (f32[4,1040]{1,0:T(4,128)S(1)}, f32[4,1040]{1,0:T(4,128)S(1)}, u32[]{:S(2)}, u32[]{:S(2)}) collective-permute-start(f32[4,1040]{1,0:T(4,128)S(1)} %dynamic-slice_bitcast_fusion.5), channel_id=1, source_target_pairs={{0,64},{1,65},{2,66},{3,67},{4,68},{5,69},{6,70},{7,71},{8,72},{9,... | collective-permute-start | bytes 49928 | tf_op jit(solution)/shard_map/ppermute | solution.py:64
Sparse Core Ops, SparseCore 0:
  9.7 67.4 all-gather.2
  79.0 63.4 all-gather.4

commit v3 on v2

--- a/solution.py
+++ b/solution.py
@@ -5,6 +5,7 @@
 
 NCLS = 16
 KSIZE = 7
+LANES = 128
 
 
 def with_halo(shard, sides, width):
@@ -21,9 +22,9 @@
 
 
 def apply_norm(rows, ln_gain):
-    mean = jnp.mean(rows, axis=-1, keepdims=True)
+    mean = jnp.mean(rows, axis=(-2, -1), keepdims=True)
     centered = rows - mean
-    var = jnp.mean(centered * centered, axis=-1, keepdims=True)
+    var = jnp.mean(centered * centered, axis=(-2, -1), keepdims=True)
     return (centered * lax.rsqrt(var + 1e-06) * ln_gain).astype(jnp.bfloat16)
 
 
@@ -73,14 +74,16 @@
 
 def on_device(features, dw_kernel, ln_gain, w_in, w_down, gamma, labels, valid):
     tiles, high, wide, width = features.shape
+    tile = (width // LANES, LANES)
     padded = with_halo(features, (("row", 1), ("col", 2)), 3).astype(jnp.float32)
-    kernel = dw_kernel.astype(jnp.float32)
-    conv = jnp.zeros((tiles, high, wide, width), jnp.float32)
+    padded = padded.reshape(padded.shape[:3] + tile)
+    kernel = dw_kernel.astype(jnp.float32).reshape((KSIZE, KSIZE) + tile)
+    conv = jnp.zeros((tiles, high, wide) + tile, jnp.float32)
     for i in range(KSIZE):
         for j in range(KSIZE):
-            conv = conv + padded[:, i : i + high, j : j + wide, :] * kernel[i, j]
+            conv = conv + padded[:, i : i + high, j : j + wide] * kernel[i, j]
     count = tiles * high * wide
-    normed = apply_norm(conv.reshape(count, width), ln_gain)
+    normed = apply_norm(conv.reshape(count, *tile), ln_gain.reshape(tile)).reshape(count, width)
     hidden = expand(normed, lax.all_gather(w_in, "col", axis=1, tiled=True))
     branch = contract(hidden, lax.all_gather(w_down, "col", axis=1, tiled=True))
     out = (features.reshape(count, width).astype(jnp.float32) + gamma * branch).astype(jnp.bfloat16)

time: 307 us -> 288 us (0.938)
  other arithmetic: 108 us -> 87.7 us
  waiting for transfers between devices: 88.7 us -> 81.3 us
  local copies, waits for them, and re-layouts: 20.7 us -> 26.7 us
    reduce_sum x2, other arithmetic: 96.4 us -> 75.9 us  [the longest x1 64.9 us: apply_norm(): mean = jnp.mean(rows, axis=(-2, -1), keepdims=True)]
    concatenate x1 -> x3, local copies, waits for them, and re-layouts: 0.02 us -> 5.34 us  [with_halo(): shard = jnp.concatenate([before, shard, after], axis=dim)]
    ppermute x2, waiting for transfers between devices: 9.92 us -> 5.03 us  [with_halo(): after = lax.ppermute(leading, axis, down)]
  transfers between devices with their start and end apart: 14 -> 14, of which waited for: 12 -> 11; matrix products, arithmetic and copies ran while one was open for 48% -> 47% of each run, Pallas kernels for 0% -> 0%
where the time goes in v3:
time: 288 us; the launch traced here: 287 us
  other arithmetic  87.7 us (30%)
  waiting for transfers between devices  81.3 us (28%)
  matrix products  53.1 us (18%)
  local copies, waits for them, and re-layouts  26.7 us (9%)
  starting transfers between devices  23.4 us (8%)
  between operations  14.8 us (5%)
    ppermute x8, waiting for transfers between devices, halving_sum(): part = keep + lax.ppermute(send, axes, pairs)  68 us
    reduce_sum x1, other arithmetic, apply_norm(): mean = jnp.mean(rows, axis=(-2, -1), keepdims=True)  64.9 us
    dot_general x1, matrix products, expand(): jnp.dot(normed, piece, preferred_element_type=jnp.float32)  37.2 us
    dot_general x1, matrix products, contract(): lax.dot_general(hidden, piece, (((1,), (1,)), ((), ())), preferred_elemen...  12.5 us
    reduce_sum x1, other arithmetic, apply_norm(): var = jnp.mean(centered * centered, axis=(-2, -1), keepdims=True)  11 us
    ppermute x8, starting transfers between devices, halving_sum(): part = keep + lax.ppermute(send, axes, pairs)  10.8 us
    ppermute x2, starting transfers between devices, with_halo(): before = lax.ppermute(last, axis, up)  6.96 us
    ppermute x2, waiting for transfers between devices, with_halo(): before = lax.ppermute(last, axis, up)  6.95 us
  transfers between devices with their start and end apart: 14, of which 11 were waited for; matrix products, arithmetic and copies ran while one was open for 47% of the time, Pallas kernels for 0%

profile of v3, /device:TPU:120, one launch (start us, length us, event | category | flops | bytes accessed | tf_op | source)
XLA Modules:
  0.0 287.0 jit_solution(4193847160994177112)
XLA Ops:
  9.8 5.0 %collective-permute-start = (bf16[3,3,16,1024]{3,2,1,0:T(8,128)(2,1)S(1)}, bf16[3,3,16,1024]{3,2,1,0:T(8,128)(2,1)S(1)}, u32[]{:S(2)}, u32[]{:S(2)}) collective-permute-start(bf16[3,3,16,1024]{3,2,1,0:T(8,128)(2,1)S(1)} %get-tuple-element.8), channel_id=1, source_target_pairs={{0,16},{16,32},{32,48},{48,64},{64,80},{80,96},{96,112},{112,128},... | collective-permute-start | bytes 884744 | tf_op jit(solution)/shard_map/ppermute | solution.py:18
  21.6 4.8 %collective-permute-done.1 = bf16[3,3,16,1024]{3,2,1,0:T(8,128)(2,1)S(1)} collective-permute-done((bf16[3,3,16,1024]{3,2,1,0:T(8,128)(2,1)S(1)}, bf16[3,3,16,1024]{3,2,1,0:T(8,128)(2,1)S(1)}, u32[]{:S(2)}, u32[]{:S(2)}) %collective-permute-start.1) | collective-permute-done | bytes 294944 | tf_op jit(solution)/shard_map/ppermute | solution.py:19
  26.7 3.0 %pad_maximum_fusion.1 = bf16[3,22,16,1024]{3,1,2,0:T(8,128)(2,1)S(1)} fusion(bf16[3,3,16,1024]{3,1,2,0:T(4,128)(2,1)S(1)} %copy.68, bf16[3,16,16,1024]{3,1,2,0:T(8,128)(2,1)} %copy.67, bf16[3,3,16,1024]{3,1,2,0:T(4,128)(2,1)S(1)} %copy.66), kind=kLoop, calls=%fused_computation.126 | loop fusion | flops 6488064 | bytes 4325376 | tf_op jit(solution)/shard_map/concatenate | solution.py:20
  31.6 3.6 %collective-permute-start.3 = (bf16[3,22,3,1024]{3,1,2,0:T(8,128)(2,1)S(1)}, bf16[3,22,3,1024]{3,1,2,0:T(8,128)(2,1)}, u32[]{:S(2)}, u32[]{:S(2)}) collective-permute-start(bf16[3,22,3,1024]{3,1,2,0:T(8,128)(2,1)S(1)} %get-tuple-element.5), channel_id=1, source_target_pairs={{1,0},{2,1},{3,2},{4,3},{5,4},{6,5},{7,6},{8,7},{9,8},{10,9},{11,1... | collective-permute-start | bytes 1216520 | tf_op jit(solution)/shard_map/ppermute | solution.py:19
  36.6 2.8 reshape.160
  39.3 6.9 %collective-permute-done.2 = bf16[3,22,3,1024]{3,1,2,0:T(8,128)(2,1)} collective-permute-done((bf16[3,22,3,1024]{3,1,2,0:T(8,128)(2,1)S(1)}, bf16[3,22,3,1024]{3,1,2,0:T(8,128)(2,1)}, u32[]{:S(2)}, u32[]{:S(2)}) %collective-permute-start.2) | collective-permute-done | bytes 405536 | tf_op jit(solution)/shard_map/ppermute | solution.py:18
  49.3 4.0 %copy_convert_fusion = f32[3,22,22,8,128]{4,3,2,1,0:T(8,128)} fusion(bf16[3,22,3,8,128]{4,3,1,2,0:T(8,128)(2,1)S(1)} %concatenate.19, bf16[3,22,16,8,128]{4,3,1,2,0:T(8,128)(2,1)} %reshape.160, bf16[3,22,3,8,128]{4,3,1,2,0:T(8,128)(2,1)S(1)} %concatenate.17), kind=kLoop, calls=%fused_computation.125 | loop fusion | flops 4460544 | bytes 8921088 | tf_op jit(solution)/shard_map/convert_element_type | solution.py:78
  53.4 64.9 %fusion.113 = (f32[3,16,16]{2,1,0:T(8,128)S(1)}, f32[3,16,16,8,128]{4,3,2,1,0:T(8,128)S(1)}) fusion(f32[8,128]{1,0:T(8,128)S(1)} %get-tuple-element.13, f32[3,22,22,8,128]{4,3,2,1,0:T(8,128)} %copy_convert_fusion, f32[8,128]{1,0:T(8,128)S(1)} %get-tuple-element.14, f32[8,128]{1,0:T(8,128)S(1)} %get-tuple-element.15, f32[8,128]{1,0:T(8,128)S(1)} %get-tuple-element.16, ...), kind=kLoop, calls=%fused_computation.242 | loop fusion | flops 77069568 | bytes 157490176 | tf_op jit(solution)/shard_map/reduce_sum | solution.py:25
  118.4 11.0 %multiply_reduce_fusion = f32[3,16,16]{2,1,0:T(8,128)S(1)} fusion(f32[3,16,16,8,128]{4,3,2,1,0:T(8,128)S(1)} %get-tuple-element.3, f32[3,16,16]{2,1,0:T(8,128)S(1)} %broadcast_multiply_fusion.1), kind=kLoop, calls=%fused_computation.123 | loop fusion | flops 2358528 | bytes 3151872 | tf_op jit(solution)/shard_map/reduce_sum | solution.py:27
  129.6 37.2 %fusion.65.clone.4 = bf16[768,4096]{1,0:T(8,128)(2,1)} fusion(bf16[1024,4096]{1,0:T(8,128)(2,1)} %all-gather.3.cloned.1.call-done, f32[96,8,8,128]{3,2,1,0:T(8,128)S(1)} %bitcast.188, f32[1024]{0:T(1024)S(1)} %copy-done.28, f32[768]{0:T(1024)S(1)} %rsqrt.12, f32[768]{0:T(1024)S(1)} %div.21), kind=kOutput, calls=%fused_computation.3.clone.clone.clone.clone.clone.clone.1 | convolution fusion | flops 6650068992 | bytes 17836032 | tf_op jit(solution)/shard_map/dot_general | solution.py:33
  166.8 12.5 %broadcast_multiply_fusion = (bf16[768,1024]{1,0:T(8,128)(2,1)S(1)}, bf16[768,1024]{1,0:T(8,128)(2,1)}) fusion(bf16[768]{0:T(1024)(128)(2,1)S(1)} %copy-done.27, bf16[1024,4096]{1,0:T(8,128)(2,1)} %all-gather.5.cloned.1.call-done, f32[1024]{0:T(1024)S(1)} %copy-done.29, bf16[768,1024]{1,0:T(8,128)(2,1)} %bitcast.190, bf16[768,4096]{1,0:T(8,128)(2,1)} %fusion.65.clone.4), kind=kOutput, calls=%fused_computation.139 | convolution fusion | flops 6446383104 | bytes 19404288 | tf_op jit(solution)/shard_map/dot_general | solution.py:38
  181.9 3.3 %fusion.66 = f32[2,512,1040]{1,2,0:T(8,128)S(1)} fusion(bf16[2,512,768]{2,1,0:T(8,128)(2,1)S(1)} %bitcast.193, bf16[768,16]{1,0:T(8,128)(2,1)S(1)} %copy-done.2, bf16[768,1024]{1,0:T(8,128)(2,1)} %get-tuple-element.62), kind=kOutput, calls=%fused_computation.130 | convolution fusion | flops 1638973440 | bytes 7430144 | tf_op jit(solution)/shard_map/dot_general | solution.py:92
  188.8 2.6 collective-permute-start.4
  191.4 4.0 %collective-permute-done.4 = f32[512,1040]{0,1:T(8,128)S(1)} collective-permute-done((f32[512,1040]{0,1:T(8,128)}, f32[512,1040]{0,1:T(8,128)S(1)}, u32[]{:S(2)}, u32[]{:S(2)}) %collective-permute-start.4) | collective-permute-done | bytes 2129952 | tf_op jit(solution)/shard_map/ppermute | solution.py:65
  195.4 3.4 %bitcast_add_fusion = f32[512,1040]{0,1:T(8,128)} fusion(f32[512,1040]{0,1:T(8,128)S(1)} %collective-permute-done.4, f32[2,512,1040]{1,2,0:T(8,128)} %copy-done, s32[]{:T(128)S(6)} %select_n.56), kind=kLoop, calls=%fused_computation.127 | loop fusion | flops 532480 | bytes 6389764 | tf_op jit(solution)/shard_map/add | solution.py:65
  198.9 2.7 reshape.149
  203.8 25.7 %collective-permute-done.5 = f32[256,1040]{0,1:T(8,128)S(1)} collective-permute-done((f32[256,1040]{0,1:T(8,128)S(1)}, f32[256,1040]{0,1:T(8,128)S(1)}, u32[]{:S(2)}, u32[]{:S(2)}) %collective-permute-start.5) | collective-permute-done | bytes 1064992 | tf_op jit(solution)/shard_map/ppermute | solution.py:65
  232.3 12.6 %collective-permute-done.6 = f32[128,1040]{0,1:T(8,128)S(1)} collective-permute-done((f32[128,1040]{0,1:T(8,128)S(1)}, f32[128,1040]{0,1:T(8,128)S(1)}, u32[]{:S(2)}, u32[]{:S(2)}) %collective-permute-start.6) | collective-permute-done | bytes 532512 | tf_op jit(solution)/shard_map/ppermute | solution.py:65
  245.3 7.6 %collective-permute-done.7 = f32[64,1040]{1,0:T(8,128)S(1)} collective-permute-done((f32[64,1040]{1,0:T(8,128)S(1)}, f32[64,1040]{1,0:T(8,128)S(1)}, u32[]{:S(2)}, u32[]{:S(2)}) %collective-permute-start.7) | collective-permute-done | bytes 266272 | tf_op jit(solution)/shard_map/ppermute | solution.py:65
  253.4 6.3 %collective-permute-done.8 = f32[32,1040]{1,0:T(8,128)S(1)} collective-permute-done((f32[32,1040]{1,0:T(8,128)S(1)}, f32[32,1040]{1,0:T(8,128)S(1)}, u32[]{:S(2)}, u32[]{:S(2)}) %collective-permute-start.8) | collective-permute-done | bytes 133152 | tf_op jit(solution)/shard_map/ppermute | solution.py:65
  259.8 5.7 %collective-permute-done.9 = f32[16,1040]{1,0:T(8,128)S(1)} collective-permute-done((f32[16,1040]{1,0:T(8,128)S(1)}, f32[16,1040]{1,0:T(8,128)S(1)}, u32[]{:S(2)}, u32[]{:S(2)}) %collective-permute-start.9) | collective-permute-done | bytes 66592 | tf_op jit(solution)/shard_map/ppermute | solution.py:65
  265.6 3.0 %collective-permute-start.10 = (f32[8,1040]{1,0:T(8,128)S(1)}, f32[8,1040]{1,0:T(8,128)S(1)}, u32[]{:S(2)}, u32[]{:S(2)}) collective-permute-start(f32[8,1040]{1,0:T(8,128)S(1)} %dynamic-slice_bitcast_fusion.4), channel_id=1, source_target_pairs={{0,128},{1,129},{2,130},{3,131},{4,132},{5,133},{6,134},{7,135},{8... | collective-permute-start | bytes 99848 | tf_op jit(solution)/shard_map/ppermute | solution.py:65
  271.2 4.3 %collective-permute-start.11 = (f32[4,1040]{1,0:T(4,128)S(1)}, f32[4,1040]{1,0:T(4,128)S(1)}, u32[]{:S(2)}, u32[]{:S(2)}) collective-permute-start(f32[4,1040]{1,0:T(4,128)S(1)} %dynamic-slice_bitcast_fusion.5), channel_id=1, source_target_pairs={{0,64},{1,65},{2,66},{3,67},{4,68},{5,69},{6,70},{7,71},{8,72},{9,... | collective-permute-start | bytes 49928 | tf_op jit(solution)/shard_map/ppermute | solution.py:65
  275.5 3.4 %collective-permute-done.11 = f32[4,1040]{1,0:T(4,128)S(1)} collective-permute-done((f32[4,1040]{1,0:T(4,128)S(1)}, f32[4,1040]{1,0:T(4,128)S(1)}, u32[]{:S(2)}, u32[]{:S(2)}) %collective-permute-start.11) | collective-permute-done | bytes 16672 | tf_op jit(solution)/shard_map/ppermute | solution.py:65
  (122 shorter events, 31.7 us)
Async XLA Ops:
  7.2 10.4 %copy-start.1 = (bf16[3,16,16,1024]{3,2,1,0:T(8,128)(2,1)S(1)}, bf16[3,16,16,1024]{3,2,1,0:T(8,128)(2,1)}, u32[]{:S(2)}) copy-start(bf16[3,16,16,1024]{3,2,1,0:T(8,128)(2,1)} %param.8) | copy-start | bytes 4718596
  7.2 12.5 %copy-start.3 = (bf16[7,7,1024]{2,1,0:T(8,128)(2,1)S(1)}, bf16[7,7,1024]{2,1,0:T(8,128)(2,1)}, u32[]{:S(2)}) copy-start(bf16[7,7,1024]{2,1,0:T(8,128)(2,1)} %param.9) | copy-start | bytes 301060
  7.2 12.6 %copy-start.4 = (s32[3,16,16]{2,1,0:T(8,128)S(1)}, s32[3,16,16]{2,1,0:T(8,128)}, u32[]{:S(2)}) copy-start(s32[3,16,16]{2,1,0:T(8,128)} %param.15) | copy-start | bytes 9220
  7.2 122.3 %all-gather.3.cloned.1.call-start = ((), (), s32[]{:S(2)}) async-start(), calls=%async_computation | async-start | bytes 8912896 | tf_op jit(solution)/shard_map/all_gather | solution.py:87
  7.9 158.8 %all-gather.5.cloned.1.call-start = ((), (), s32[]{:S(2)}) async-start(), calls=%async_computation.1 | async-start | bytes 8912896 | tf_op jit(solution)/shard_map/all_gather | solution.py:88
  9.8 11.5 %collective-permute-start = (bf16[3,3,16,1024]{3,2,1,0:T(8,128)(2,1)S(1)}, bf16[3,3,16,1024]{3,2,1,0:T(8,128)(2,1)S(1)}, u32[]{:S(2)}, u32[]{:S(2)}) collective-permute-start(bf16[3,3,16,1024]{3,2,1,0:T(8,128)(2,1)S(1)} %get-tuple-element.8), channel_id=1, source_target_pairs={{0,16},{16,32},{32,48},{48,64},{64,80},{80,96},{96,112},{112,128},... | collective-permute-start | bytes 884744 | tf_op jit(solution)/shard_map/ppermute | solution.py:18
  14.8 11.6 %collective-permute-start.1 = (bf16[3,3,16,1024]{3,2,1,0:T(8,128)(2,1)S(1)}, bf16[3,3,16,1024]{3,2,1,0:T(8,128)(2,1)S(1)}, u32[]{:S(2)}, u32[]{:S(2)}) collective-permute-start(bf16[3,3,16,1024]{3,2,1,0:T(8,128)(2,1)S(1)} %get-tuple-element.9), channel_id=1, source_target_pairs={{16,0},{32,16},{48,32},{64,48},{80,64},{96,80},{112,96},{128,112},... | collective-permute-start | bytes 884744 | tf_op jit(solution)/shard_map/ppermute | solution.py:19
  29.7 16.6 %collective-permute-start.2 = (bf16[3,22,3,1024]{3,1,2,0:T(8,128)(2,1)S(1)}, bf16[3,22,3,1024]{3,1,2,0:T(8,128)(2,1)}, u32[]{:S(2)}, u32[]{:S(2)}) collective-permute-start(bf16[3,22,3,1024]{3,1,2,0:T(8,128)(2,1)S(1)} %get-tuple-element.4), channel_id=1, source_target_pairs={{0,1},{1,2},{2,3},{3,4},{4,5},{5,6},{6,7},{7,8},{8,9},{9,10},{10,1... | collective-permute-start | bytes 1216520 | tf_op jit(solution)/shard_map/ppermute | solution.py:18
  31.6 16.1 %collective-permute-start.3 = (bf16[3,22,3,1024]{3,1,2,0:T(8,128)(2,1)S(1)}, bf16[3,22,3,1024]{3,1,2,0:T(8,128)(2,1)}, u32[]{:S(2)}, u32[]{:S(2)}) collective-permute-start(bf16[3,22,3,1024]{3,1,2,0:T(8,128)(2,1)S(1)} %get-tuple-element.5), channel_id=1, source_target_pairs={{1,0},{2,1},{3,2},{4,3},{5,4},{6,5},{7,6},{8,7},{9,8},{10,9},{11,1... | collective-permute-start | bytes 1216520 | tf_op jit(solution)/shard_map/ppermute | solution.py:19
  49.1 4.2 %copy-start.5 = (f32[8,128]{1,0:T(8,128)S(1)}, f32[8,128]{1,0:T(8,128)}, u32[]{:S(2)}) copy-start(f32[8,128]{1,0:T(8,128)} %get-tuple-element.58) | copy-start | bytes 12292
  49.1 4.2 %copy-start.6 = (f32[8,128]{1,0:T(8,128)S(1)}, f32[8,128]{1,0:T(8,128)}, u32[]{:S(2)}) copy-start(f32[8,128]{1,0:T(8,128)} %get-tuple-element.59) | copy-start | bytes 12292
  49.1 4.2 %copy-start.7 = (f32[8,128]{1,0:T(8,128)S(1)}, f32[8,128]{1,0:T(8,128)}, u32[]{:S(2)}) copy-start(f32[8,128]{1,0:T(8,128)} %get-tuple-element.60) | copy-start | bytes 12292
  49.1 4.2 %copy-start.8 = (f32[8,128]{1,0:T(8,128)S(1)}, f32[8,128]{1,0:T(8,128)}, u32[]{:S(2)}) copy-start(f32[8,128]{1,0:T(8,128)} %get-tuple-element.31) | copy-start | bytes 12292
  118.3 11.2 %copy-start.28 = (f32[1024]{0:T(1024)S(1)}, f32[1024]{0:T(1024)}, u32[]{:S(2)}) copy-start(f32[1024]{0:T(1024)} %param.10) | copy-start | bytes 12292
  129.5 37.2 %copy-start.27 = (bf16[768]{0:T(1024)(128)(2,1)S(1)}, bf16[768]{0:T(1024)(128)(2,1)}, u32[]{:S(2)}) copy-start(bf16[768]{0:T(1024)(128)(2,1)} %convert_element_type.45) | copy-start | bytes 4612
  129.5 37.2 %copy-start.29 = (f32[1024]{0:T(1024)S(1)}, f32[1024]{0:T(1024)}, u32[]{:S(2)}) copy-start(f32[1024]{0:T(1024)} %param.13) | copy-start | bytes 12292
  188.8 6.7 %collective-permute-start.4 = (f32[512,1040]{0,1:T(8,128)}, f32[512,1040]{0,1:T(8,128)S(1)}, u32[]{:S(2)}, u32[]{:S(2)}) collective-permute-start(f32[512,1040]{0,1:T(8,128)} %dynamic-slice_bitcast_fusion), channel_id=1, source_target_pairs={{0,1},{1,0},{2,3},{3,2},{4,5},{5,4},{6,7},{7,6},{8,9},{9,8},{10,11... | collective-permute-start | bytes 6389768 | tf_op jit(solution)/shard_map/ppermute | solution.py:65
  203.5 25.9 %collective-permute-start.5 = (f32[256,1040]{0,1:T(8,128)S(1)}, f32[256,1040]{0,1:T(8,128)S(1)}, u32[]{:S(2)}, u32[]{:S(2)}) collective-permute-start(f32[256,1040]{0,1:T(8,128)S(1)} %bitcast.196), channel_id=1, source_target_pairs={{0,2},{1,3},{2,0},{3,1},{4,6},{5,7},{6,4},{7,5},{8,10},{9,11},{10,... | collective-permute-start | bytes 3194888 | tf_op jit(solution)/shard_map/ppermute | solution.py:65
  231.3 13.6 %collective-permute-start.6 = (f32[128,1040]{0,1:T(8,128)S(1)}, f32[128,1040]{0,1:T(8,128)S(1)}, u32[]{:S(2)}, u32[]{:S(2)}) collective-permute-start(f32[128,1040]{0,1:T(8,128)S(1)} %bitcast.199), channel_id=1, source_target_pairs={{0,8},{1,9},{2,10},{3,11},{4,12},{5,13},{6,14},{7,15},{8,0},{9,1},... | collective-permute-start | bytes 1597448 | tf_op jit(solution)/shard_map/ppermute | solution.py:65
  245.2 7.7 %collective-permute-start.7 = (f32[64,1040]{1,0:T(8,128)S(1)}, f32[64,1040]{1,0:T(8,128)S(1)}, u32[]{:S(2)}, u32[]{:S(2)}) collective-permute-start(f32[64,1040]{1,0:T(8,128)S(1)} %dynamic-slice_bitcast_fusion.1), channel_id=1, source_target_pairs={{0,16},{1,17},{2,18},{3,19},{4,20},{5,21},{6,22},{7,23},{8,24},{9,... | collective-permute-start | bytes 798728 | tf_op jit(solution)/shard_map/ppermute | solution.py:65
  253.0 6.7 %collective-permute-start.8 = (f32[32,1040]{1,0:T(8,128)S(1)}, f32[32,1040]{1,0:T(8,128)S(1)}, u32[]{:S(2)}, u32[]{:S(2)}) collective-permute-start(f32[32,1040]{1,0:T(8,128)S(1)} %dynamic-slice_bitcast_fusion.2), channel_id=1, source_target_pairs={{0,4},{1,5},{2,6},{3,7},{4,0},{5,1},{6,2},{7,3},{8,12},{9,13},{10,... | collective-permute-start | bytes 399368 | tf_op jit(solution)/shard_map/ppermute | solution.py:65
  259.7 5.9 %collective-permute-start.9 = (f32[16,1040]{1,0:T(8,128)S(1)}, f32[16,1040]{1,0:T(8,128)S(1)}, u32[]{:S(2)}, u32[]{:S(2)}) collective-permute-start(f32[16,1040]{1,0:T(8,128)S(1)} %dynamic-slice_bitcast_fusion.3), channel_id=1, source_target_pairs={{0,32},{1,33},{2,34},{3,35},{4,36},{5,37},{6,38},{7,39},{8,40},{9,... | collective-permute-start | bytes 199688 | tf_op jit(solution)/shard_map/ppermute | solution.py:65
  265.6 5.5 %collective-permute-start.10 = (f32[8,1040]{1,0:T(8,128)S(1)}, f32[8,1040]{1,0:T(8,128)S(1)}, u32[]{:S(2)}, u32[]{:S(2)}) collective-permute-start(f32[8,1040]{1,0:T(8,128)S(1)} %dynamic-slice_bitcast_fusion.4), channel_id=1, source_target_pairs={{0,128},{1,129},{2,130},{3,131},{4,132},{5,133},{6,134},{7,135},{8... | collective-permute-start | bytes 99848 | tf_op jit(solution)/shard_map/ppermute | solution.py:65
  271.2 7.8 %collective-permute-start.11 = (f32[4,1040]{1,0:T(4,128)S(1)}, f32[4,1040]{1,0:T(4,128)S(1)}, u32[]{:S(2)}, u32[]{:S(2)}) collective-permute-start(f32[4,1040]{1,0:T(4,128)S(1)} %dynamic-slice_bitcast_fusion.5), channel_id=1, source_target_pairs={{0,64},{1,65},{2,66},{3,67},{4,68},{5,69},{6,70},{7,71},{8,72},{9,... | collective-permute-start | bytes 49928 | tf_op jit(solution)/shard_map/ppermute | solution.py:65
  (20 other events, 78.2 us)
Sparse Core Ops, SparseCore 0:
  9.8 67.4 all-gather.2
  79.0 62.2 all-gather.4
